TPU v7x, 256 devices: a whole 4x4x8 slice. The times are simulated.
256 devices in a mesh: gx: 16 (over z, core), gy: 16 (over y, x).
Axes of the slice: x: 4, y: 4, z: 8, core: 2. Of those that a mesh axis runs over, the one named last changes fastest.
Arguments:
- right_side: float32 [256, 128, 1024], P('gx', 'gy'), may hold values from -340 to 340
- start_guess: float32 [256, 128, 1024], P('gx', 'gy'), may hold values from -1.8 to 1.8
- couple_x: float32 [256, 128, 64], P('gx', 'gy'), may hold values from 0.3 to 3
- couple_y: float32 [256, 128, 64], P('gx', 'gy'), may hold values from 0.3 to 3
- couple_z: float32 [256, 128, 64], P('gx', 'gy'), may hold values from 0.3 to 3
- reaction: float32 [256, 128, 64], P('gx', 'gy'), may hold values from 0.01 to 0.1
Outputs:
- solution: float32 [256, 128, 1024], P('gx', 'gy')
- residual: float32 [256, 128, 1024], P('gx', 'gy')
All inputs are finite; a program needn't handle non-finite values.
Results may differ from a plain program's by a relative error of at most 0.0003.
Values sent between devices are 32-bit elements; how exact they have to be, the bound alone decides.
No kernel may reach another device: no remote copies, remote signals or barrier semaphores. Data moves between devices by JAX's collectives and lax.ppermute only.
A program may use at most 64 MiB of HBM per device.

v0:
```python
import jax
import jax.numpy as jnp
from jax import lax
from jax.sharding import PartitionSpec as P

ITERS = 2
SWEEPS = 4
FACT_SWEEPS = 3
HIGH = lax.Precision.HIGHEST


def passed_along(block, axis, distance):
    devices = range(lax.axis_size(axis))
    route = [(i - distance, i) for i in devices if i - distance in devices]
    return lax.ppermute(block, axis, route)


def padded_2(block, sides, width):
    for axis, dim in sides:
        count = lax.axis_size(axis)
        forward = [(i, i + 1) for i in range(count - 1)]
        backward = [(target, source) for source, target in forward]
        low = lax.ppermute(
            lax.slice_in_dim(block, block.shape[dim] - width, None, axis=dim), axis, forward
        )
        high = lax.ppermute(lax.slice_in_dim(block, 0, width, axis=dim), axis, backward)
        block = jnp.concatenate([low, block, high], axis=dim)
    return block


def low_shift(values, along):
    count = values.shape[along]
    blank = jnp.zeros_like(lax.slice_in_dim(values, 0, 1, axis=along))
    return jnp.concatenate([blank, lax.slice_in_dim(values, 0, count - 1, axis=along)], axis=along)


def up_shift(values, along):
    count = values.shape[along]
    blank = jnp.zeros_like(lax.slice_in_dim(values, 0, 1, axis=along))
    return jnp.concatenate([lax.slice_in_dim(values, 1, count, axis=along), blank], axis=along)


def block_gram(former, latter, count_rhs):
    cells = former.shape[0] * former.shape[1]
    left = former.reshape(cells, count_rhs, -1)
    right = latter.reshape(cells, count_rhs, -1)
    return jnp.einsum("psz,ptz->st", left, right, precision=HIGH)


def mix_block(values, matrix):
    rows_x, rows_y, flat_len = values.shape
    count_rhs = matrix.shape[0]
    split = values.reshape(rows_x * rows_y, count_rhs, flat_len // count_rhs)
    return jnp.einsum("psz,st->ptz", split, matrix, precision=HIGH).reshape(
        rows_x, rows_y, flat_len
    )


def chol_factor(gram_mat):
    low_factor = jnp.linalg.cholesky(gram_mat)
    eye_mat = jnp.eye(gram_mat.shape[0], dtype=gram_mat.dtype)
    inverse = lax.linalg.triangular_solve(low_factor, eye_mat, left_side=True, lower=True)
    return (low_factor.T, inverse.T)


def solve_small(columns, first_factor):
    hessen = jnp.concatenate(columns, axis=1)
    count_rhs = first_factor.shape[0]
    target = jnp.dot(hessen[:count_rhs].T, first_factor, precision=HIGH)
    normal = jnp.dot(hessen.T, hessen, precision=HIGH)
    low_factor = jnp.linalg.cholesky(normal)
    partial_sol = lax.linalg.triangular_solve(low_factor, target, left_side=True, lower=True)
    return lax.linalg.triangular_solve(
        low_factor, partial_sol, left_side=True, lower=True, transpose_a=True
    )


def body(right_side, start_guess, couple_x, couple_y, couple_z, reaction):
    rows_x, rows_y, flat_len = right_side.shape
    layers = couple_z.shape[2]
    count_rhs = flat_len // layers
    depth = jnp.arange(flat_len, dtype=jnp.int32) % layers
    keep_first = (depth != 0).astype(jnp.float32)
    keep_last = (depth != layers - 1).astype(jnp.float32)

    def low_z(values):
        return low_shift(values, 2) * keep_first

    def up_z(values):
        return up_shift(values, 2) * keep_last

    def tiled(values):
        return jnp.tile(values, (1, 1, count_rhs))

    edge_x = passed_along(couple_x[-1:], "gx", 1)
    edge_y = passed_along(couple_y[:, -1:], "gy", 1)
    after_x = tiled(couple_x)
    after_y = tiled(couple_y)
    after_z = tiled(couple_z)
    before_x = tiled(jnp.concatenate([edge_x, couple_x[:-1]], axis=0))
    before_y = tiled(jnp.concatenate([edge_y, couple_y[:, :-1]], axis=1))
    before_z = low_z(after_z)
    diagonal = tiled(reaction) + after_x + before_x + after_y + before_y + after_z + before_z

    def apply_op(values):
        padded = padded_2(values, (("gx", 0), ("gy", 1)), 1)
        centre = padded[1:-1, 1:-1]
        return (
            diagonal * centre
            - after_x * padded[2:, 1:-1]
            - before_x * padded[:-2, 1:-1]
            - after_y * padded[1:-1, 2:]
            - before_y * padded[1:-1, :-2]
            - after_z * up_z(centre)
            - before_z * low_z(centre)
        )

    lows = (low_shift(after_x, 0), low_shift(after_y, 1), before_z)
    ups = (
        up_shift(jnp.ones_like(after_x), 0) * after_x,
        up_shift(jnp.ones_like(after_y), 1) * after_y,
        after_z,
    )
    pivots = diagonal
    for repeat in range(FACT_SWEEPS):
        inv_now = 1.0 / pivots
        pivots = (
            diagonal
            - lows[0] * lows[0] * low_shift(inv_now, 0)
            - lows[1] * lows[1] * low_shift(inv_now, 1)
            - lows[2] * lows[2] * low_z(inv_now)
        )
    inv_piv = 1.0 / pivots

    def total_gram(former, latter):
        return lax.psum(block_gram(former, latter, count_rhs), ("gx", "gy"))

    start_res = right_side - apply_op(start_guess)
    first_factor, first_inv = chol_factor(total_gram(start_res, start_res))
    basis_set = [mix_block(start_res, first_inv)]
    precond_set = []
    image_set = []
    columns = []
    for column in range(ITERS):
        source = basis_set[column]
        lower_sol = inv_piv * source
        for precondition_repeat in range(SWEEPS):
            lower_sol = inv_piv * (
                source
                + lows[0] * low_shift(lower_sol, 0)
                + lows[1] * low_shift(lower_sol, 1)
                + lows[2] * low_z(lower_sol)
            )
        upper_sol = lower_sol
        for precondition_repeat in range(SWEEPS):
            upper_sol = lower_sol + inv_piv * (
                ups[0] * up_shift(upper_sol, 0)
                + ups[1] * up_shift(upper_sol, 1)
                + ups[2] * up_z(upper_sol)
            )
        image = apply_op(upper_sol)
        precond_set.append(upper_sol)
        image_set.append(image)
        local_proj = jnp.stack([block_gram(member, image, count_rhs) for member in basis_set])
        stacked = lax.psum(local_proj, ("gx", "gy"))
        projections = [stacked[member] for member in range(len(basis_set))]
        removed = mix_block(basis_set[0], projections[0])
        for member in range(1, len(basis_set)):
            removed = removed + mix_block(basis_set[member], projections[member])
        perp = image - removed
        next_factor, next_inv = chol_factor(total_gram(perp, perp))
        if column + 1 < ITERS:
            basis_set.append(mix_block(perp, next_inv))
        blank = jnp.zeros(((ITERS - 1 - column) * count_rhs, count_rhs), dtype=next_factor.dtype)
        columns.append(jnp.concatenate(projections + [next_factor, blank], axis=0))
    coeffs = solve_small(columns, first_factor)
    solution = start_guess
    for column in range(ITERS):
        solution = solution + mix_block(
            precond_set[column], coeffs[column * count_rhs : (column + 1) * count_rhs]
        )
    residual = right_side - apply_op(solution)
    return (solution, residual)


def solution(mesh):
    return jax.shard_map(
        body,
        mesh=mesh,
        in_specs=(
            P("gx", "gy", None),
            P("gx", "gy", None),
            P("gx", "gy", None),
            P("gx", "gy", None),
            P("gx", "gy", None),
            P("gx", "gy", None),
        ),
        out_specs=(P("gx", "gy", None), P("gx", "gy", None)),
        check_vma=False,
    )
```

profile of v0, /device:TPU:40, one launch (start us, length us, event | category | flops | bytes accessed | tf_op | source)
XLA Modules:
  0.0 608.5 jit_solution(9430777300080090725)
XLA Ops:
  3.4 3.6 collective-permute-start.2
  9.3 3.4 collective-permute-start.1
  29.7 4.6 collective-permute-start.4
  39.6 3.6 collective-permute-done.5
  43.2 3.8 fusion.36
  49.3 3.1 convolution_bitcast_fusion.12
  52.4 2.5 copy.35
  57.6 77.3 %psum.35 = f32[16,16]{0,1:T(8,128)S(1)} all-reduce(f32[16,16]{0,1:T(8,128)S(1)} %convolution_bitcast_fusion.12), channel_id=1, replica_groups=mesh['gx'=16,'gy'=16] {'gx','gy'}, use_global_device_ids=true, to_apply=%region_0.1 | all-reduce | flops 256 | bytes 2048 | tf_op jit(solution)/shard_map/psum | solution.py:136
  153.0 2.8 collective-permute-start.6
  157.7 3.3 collective-permute-done.7
  161.1 4.6 collective-permute-start.8
  168.1 6.2 %collective-permute-done.9 = f32[18,1,1024]{2,1,0:T(1,128)S(1)} collective-permute-done((f32[18,1,1024]{2,1,0:T(1,128)S(1)}, f32[18,1,1024]{2,1,0:T(1,128)S(1)}, u32[]{:S(2)}, u32[]{:S(2)}) %collective-permute-start.9) | collective-permute-done | bytes 73760 | tf_op jit(solution)/shard_map/ppermute | solution.py:23
  178.0 2.5 copy.37
  182.5 71.4 %psum.36 = f32[16,16]{0,1:T(8,128)S(1)} all-reduce(f32[16,16]{0,1:T(8,128)S(1)} %convolution_bitcast_fusion.10), channel_id=1, replica_groups=mesh['gx'=16,'gy'=16] {'gx','gy'}, use_global_device_ids=true, to_apply=%region_3.6 | all-reduce | flops 256 | bytes 2048 | tf_op jit(solution)/shard_map/psum | solution.py:165
  256.3 2.5 copy.39
  265.4 2.5 copy.44
  268.0 3.1 convolution_bitcast_fusion.9
  271.0 74.0 %psum.37 = f32[16,16]{0,1:T(8,128)S(1)} all-reduce(f32[16,16]{0,1:T(8,128)S(1)} %convolution_bitcast_fusion.9), channel_id=1, replica_groups=mesh['gx'=16,'gy'=16] {'gx','gy'}, use_global_device_ids=true, to_apply=%region_4.7 | all-reduce | flops 256 | bytes 2048 | tf_op jit(solution)/shard_map/psum | solution.py:136
  351.8 2.5 copy.45
  364.9 2.9 collective-permute-start.10
  372.3 2.6 copy.56
  375.0 4.6 collective-permute-start.12
  384.0 2.5 copy.58
  388.1 2.9 fusion.15
  393.3 2.6 copy.46
  398.7 75.0 %psum.38 = f32[2,16,16]{1,2,0:T(8,128)S(1)} all-reduce(f32[2,16,16]{1,2,0:T(8,128)S(1)} %pad_maximum_fusion.39), channel_id=1, replica_groups=mesh['gx'=16,'gy'=16] {'gx','gy'}, use_global_device_ids=true, to_apply=%region_5.8 | all-reduce | flops 512 | bytes 4096 | tf_op jit(solution)/shard_map/psum | solution.py:165
  483.3 3.1 convolution_bitcast_fusion.5
  486.5 74.9 %psum.39 = f32[16,16]{0,1:T(8,128)S(1)} all-reduce(f32[16,16]{0,1:T(8,128)S(1)} %convolution_bitcast_fusion.5), channel_id=1, replica_groups=mesh['gx'=16,'gy'=16] {'gx','gy'}, use_global_device_ids=true, to_apply=%region_6.9 | all-reduce | flops 256 | bytes 2048 | tf_op jit(solution)/shard_map/psum | solution.py:136
  565.4 2.9 cholesky.41
  590.7 2.8 collective-permute-done.15
  593.6 4.7 collective-permute-start.16
  600.6 6.2 %collective-permute-done.17 = f32[18,1,1024]{2,1,0:T(1,128)S(1)} collective-permute-done((f32[18,1,1024]{2,1,0:T(1,128)S(1)}, f32[18,1,1024]{2,1,0:T(1,128)S(1)}, u32[]{:S(2)}, u32[]{:S(2)}) %collective-permute-start.17) | collective-permute-done | bytes 73760 | tf_op jit(solution)/shard_map/ppermute | solution.py:23
  (240 shorter events, 141.7 us)
Async XLA Ops:
  0.6 6.4 %copy-start.24 = (f32[16,8,64]{2,1,0:T(8,128)S(1)}, f32[16,8,64]{2,1,0:T(8,128)}, u32[]{:S(2)}) copy-start(f32[16,8,64]{2,1,0:T(8,128)} %param.11) | copy-start | bytes 98308
  0.6 8.6 %copy-start.23 = (f32[16,8,64]{2,1,0:T(8,128)S(1)}, f32[16,8,64]{2,1,0:T(8,128)}, u32[]{:S(2)}) copy-start(f32[16,8,64]{2,1,0:T(8,128)} %param.12) | copy-start | bytes 98308
  1.5 27.3 %collective-permute-start.3 = (f32[1,8,1024]{2,1,0:T(8,128)S(1)}, f32[1,8,1024]{2,1,0:T(8,128)S(1)}, u32[]{:S(2)}, u32[]{:S(2)}) collective-permute-start(f32[1,8,1024]{2,1,0:T(8,128)S(1)} %get-tuple-element.31), channel_id=1, source_target_pairs={{0,16},{16,32},{32,48},{48,64},{64,80},{80,96},{96,112},{112,128},... | collective-permute-start | bytes 98312 | tf_op jit(solution)/shard_map/ppermute | solution.py:23
  3.4 25.4 %collective-permute-start.2 = (f32[1,8,1024]{2,1,0:T(8,128)S(1)}, f32[1,8,1024]{2,1,0:T(8,128)S(1)}, u32[]{:S(2)}, u32[]{:S(2)}) collective-permute-start(f32[1,8,1024]{2,1,0:T(8,128)S(1)} %get-tuple-element.30), channel_id=1, source_target_pairs={{16,0},{32,16},{48,32},{64,48},{80,64},{96,80},{112,96},{128,112},... | collective-permute-start | bytes 98312 | tf_op jit(solution)/shard_map/ppermute | solution.py:26
  7.1 18.2 %collective-permute-start = (f32[1,8,64]{2,1,0:T(8,128)S(1)}, f32[1,8,64]{2,1,0:T(8,128)S(1)}, u32[]{:S(2)}, u32[]{:S(2)}) collective-permute-start(f32[1,8,64]{2,1,0:T(8,128)S(1)} %slice.369), channel_id=1, source_target_pairs={{0,16},{16,32},{32,48},{48,64},{64,80},{80,96},{96,112},{112,128},... | collective-permute-start | bytes 6152 | tf_op jit(solution)/shard_map/ppermute | solution.py:15
  9.3 26.9 %collective-permute-start.1 = (f32[16,1,64]{2,1,0:T(1,128)S(1)}, f32[16,1,64]{2,1,0:T(1,128)S(1)}, u32[]{:S(2)}, u32[]{:S(2)}) collective-permute-start(f32[16,1,64]{2,1,0:T(1,128)S(1)} %slice.371), channel_id=1, source_target_pairs={{0,1},{1,2},{2,3},{3,4},{4,5},{5,6},{6,7},{7,8},{8,9},{9,10},{10,1... | collective-permute-start | bytes 12296 | tf_op jit(solution)/shard_map/ppermute | solution.py:15
  26.3 2.4 copy-start.7
  29.7 9.9 %collective-permute-start.4 = (f32[18,1,1024]{2,1,0:T(1,128)S(1)}, f32[18,1,1024]{2,1,0:T(1,128)S(1)}, u32[]{:S(2)}, u32[]{:S(2)}) collective-permute-start(f32[18,1,1024]{2,1,0:T(1,128)S(1)} %get-tuple-element.14), channel_id=1, source_target_pairs={{1,0},{2,1},{3,2},{4,3},{5,4},{6,5},{7,6},{8,7},{9,8},{10,9},{11,1... | collective-permute-start | bytes 221192 | tf_op jit(solution)/shard_map/ppermute | solution.py:26
  34.3 8.9 %collective-permute-start.5 = (f32[18,1,1024]{2,1,0:T(1,128)S(1)}, f32[18,1,1024]{2,1,0:T(1,128)S(1)}, u32[]{:S(2)}, u32[]{:S(2)}) collective-permute-start(f32[18,1,1024]{2,1,0:T(1,128)S(1)} %get-tuple-element.15), channel_id=1, source_target_pairs={{0,1},{1,2},{2,3},{3,4},{4,5},{5,6},{6,7},{7,8},{8,9},{9,10},{10,1... | collective-permute-start | bytes 221192 | tf_op jit(solution)/shard_map/ppermute | solution.py:23
  152.9 21.3 %copy-start = (f32[16,8,1024]{2,1,0:T(8,128)}, f32[16,8,1024]{2,1,0:T(8,128)S(1)}, u32[]{:S(2)}) copy-start(f32[16,8,1024]{2,1,0:T(8,128)S(1)} %multiply_add_fusion.4) | copy-start | bytes 1572868
  153.0 4.8 collective-permute-start.6
  155.8 5.2 collective-permute-start.7
  161.1 6.9 %collective-permute-start.8 = (f32[18,1,1024]{2,1,0:T(1,128)S(1)}, f32[18,1,1024]{2,1,0:T(1,128)S(1)}, u32[]{:S(2)}, u32[]{:S(2)}) collective-permute-start(f32[18,1,1024]{2,1,0:T(1,128)S(1)} %get-tuple-element.12), channel_id=1, source_target_pairs={{1,0},{2,1},{3,2},{4,3},{5,4},{6,5},{7,6},{8,7},{9,8},{10,9},{11,1... | collective-permute-start | bytes 221192 | tf_op jit(solution)/shard_map/ppermute | solution.py:26
  165.8 8.5 %copy-start.10 = (f32[16,8,1024]{2,1,0:T(8,128)S(1)}, f32[16,8,1024]{2,1,0:T(8,128)}, u32[]{:S(2)}) copy-start(f32[16,8,1024]{2,1,0:T(8,128)} %tile.63) | copy-start | bytes 1572868
  165.8 8.5 %copy-start.12 = (f32[16,8,1024]{2,1,0:T(8,128)S(1)}, f32[16,8,1024]{2,1,0:T(8,128)}, u32[]{:S(2)}) copy-start(f32[16,8,1024]{2,1,0:T(8,128)} %tile.67) | copy-start | bytes 1572868
  165.8 8.5 %collective-permute-start.9 = (f32[18,1,1024]{2,1,0:T(1,128)S(1)}, f32[18,1,1024]{2,1,0:T(1,128)S(1)}, u32[]{:S(2)}, u32[]{:S(2)}) collective-permute-start(f32[18,1,1024]{2,1,0:T(1,128)S(1)} %get-tuple-element.13), channel_id=1, source_target_pairs={{0,1},{1,2},{2,3},{3,4},{4,5},{5,6},{6,7},{7,8},{8,9},{9,10},{10,1... | collective-permute-start | bytes 221192 | tf_op jit(solution)/shard_map/ppermute | solution.py:23
  364.9 10.0 %collective-permute-start.10 = (f32[1,8,1024]{2,1,0:T(8,128)S(1)}, f32[1,8,1024]{2,1,0:T(8,128)S(1)}, u32[]{:S(2)}, u32[]{:S(2)}) collective-permute-start(f32[1,8,1024]{2,1,0:T(8,128)S(1)} %get-tuple-element.23), channel_id=1, source_target_pairs={{16,0},{32,16},{48,32},{64,48},{80,64},{96,80},{112,96},{128,112},... | collective-permute-start | bytes 98312 | tf_op jit(solution)/shard_map/ppermute | solution.py:26
  367.9 7.0 %collective-permute-start.11 = (f32[1,8,1024]{2,1,0:T(8,128)S(1)}, f32[1,8,1024]{2,1,0:T(8,128)S(1)}, u32[]{:S(2)}, u32[]{:S(2)}) collective-permute-start(f32[1,8,1024]{2,1,0:T(8,128)S(1)} %get-tuple-element.22), channel_id=1, source_target_pairs={{0,16},{16,32},{32,48},{48,64},{64,80},{80,96},{96,112},{112,128},... | collective-permute-start | bytes 98312 | tf_op jit(solution)/shard_map/ppermute | solution.py:23
  372.3 2.6 copy-start.2
  375.0 11.5 %collective-permute-start.12 = (f32[18,1,1024]{2,1,0:T(1,128)S(1)}, f32[18,1,1024]{2,1,0:T(1,128)S(1)}, u32[]{:S(2)}, u32[]{:S(2)}) collective-permute-start(f32[18,1,1024]{2,1,0:T(1,128)S(1)} %get-tuple-element.10), channel_id=1, source_target_pairs={{1,0},{2,1},{3,2},{4,3},{5,4},{6,5},{7,6},{8,7},{9,8},{10,9},{11,1... | collective-permute-start | bytes 221192 | tf_op jit(solution)/shard_map/ppermute | solution.py:26
  379.6 8.4 %collective-permute-start.13 = (f32[18,1,1024]{2,1,0:T(1,128)S(1)}, f32[18,1,1024]{2,1,0:T(1,128)S(1)}, u32[]{:S(2)}, u32[]{:S(2)}) collective-permute-start(f32[18,1,1024]{2,1,0:T(1,128)S(1)} %get-tuple-element.11), channel_id=1, source_target_pairs={{0,1},{1,2},{2,3},{3,4},{4,5},{5,6},{6,7},{7,8},{8,9},{9,10},{10,1... | collective-permute-start | bytes 221192 | tf_op jit(solution)/shard_map/ppermute | solution.py:23
  393.3 2.6 copy-start.4
  476.7 2.4 copy-start.17
  483.3 89.2 %copy-start.20 = (f32[128,16,64]{0,1,2:T(8,128)S(1)}, f32[128,16,64]{0,1,2:T(8,128)}, u32[]{:S(2)}) copy-start(f32[128,16,64]{0,1,2:T(8,128)} %copy.56) | copy-start | bytes 1572868
  586.3 20.5 %copy-start.9 = (f32[16,8,1024]{2,1,0:T(8,128)}, f32[16,8,1024]{2,1,0:T(8,128)S(1)}, u32[]{:S(2)}) copy-start(f32[16,8,1024]{2,1,0:T(8,128)S(1)} %add_add_fusion) | copy-start | bytes 1572868
  586.3 4.3 collective-permute-start.14
  588.3 5.2 collective-permute-start.15
  593.6 7.0 %collective-permute-start.16 = (f32[18,1,1024]{2,1,0:T(1,128)S(1)}, f32[18,1,1024]{2,1,0:T(1,128)S(1)}, u32[]{:S(2)}, u32[]{:S(2)}) collective-permute-start(f32[18,1,1024]{2,1,0:T(1,128)S(1)} %get-tuple-element.8), channel_id=1, source_target_pairs={{1,0},{2,1},{3,2},{4,3},{5,4},{6,5},{7,6},{8,7},{9,8},{10,9},{11,1... | collective-permute-start | bytes 221192 | tf_op jit(solution)/shard_map/ppermute | solution.py:26
  598.2 8.5 %copy-start.11 = (f32[16,8,1024]{2,1,0:T(8,128)S(1)}, f32[16,8,1024]{2,1,0:T(8,128)}, u32[]{:S(2)}) copy-start(f32[16,8,1024]{2,1,0:T(8,128)} %tile.63) | copy-start | bytes 1572868
  598.3 8.5 %copy-start.13 = (f32[16,8,1024]{2,1,0:T(8,128)S(1)}, f32[16,8,1024]{2,1,0:T(8,128)}, u32[]{:S(2)}) copy-start(f32[16,8,1024]{2,1,0:T(8,128)} %tile.67) | copy-start | bytes 1572868
  598.3 8.5 %copy-start.19 = (f32[16,8,1024]{2,1,0:T(8,128)S(1)}, f32[16,8,1024]{2,1,0:T(8,128)}, u32[]{:S(2)}) copy-start(f32[16,8,1024]{2,1,0:T(8,128)} %param.9) | copy-start | bytes 1572868
  598.3 8.5 %collective-permute-start.17 = (f32[18,1,1024]{2,1,0:T(1,128)S(1)}, f32[18,1,1024]{2,1,0:T(1,128)S(1)}, u32[]{:S(2)}, u32[]{:S(2)}) collective-permute-start(f32[18,1,1024]{2,1,0:T(1,128)S(1)} %get-tuple-element.9), channel_id=1, source_target_pairs={{0,1},{1,2},{2,3},{3,4},{4,5},{5,6},{6,7},{7,8},{8,9},{9,10},{10,1... | collective-permute-start | bytes 221192 | tf_op jit(solution)/shard_map/ppermute | solution.py:23
  (13 other events, 18.1 us)
where the time goes:
time: 617 us; the launch traced here: 609 us
  blocking collectives  373 us (60%)
  local copies, waits for them, and re-layouts  87.7 us (14%)
  starting transfers between devices  51.7 us (8%)
  other arithmetic  44.9 us (7%)
  matrix products  26 us (4%)
  waiting for transfers between devices  23.7 us (4%)
    psum x3, blocking collectives, total_gram(): return lax.psum(block_gram(former, latter, count_rhs), ('gx', 'gy'))  226 us
    psum x2, blocking collectives, body(): stacked = lax.psum(local_proj, ('gx', 'gy'))  146 us
    ppermute x8, starting transfers between devices, padded_2(): lax.ppermute(lax.slice_in_dim(block, 0, width, axis=dim), axis, backward)  29.8 us
    ppermute x8, waiting for transfers between devices, padded_2(): lax.ppermute(lax.slice_in_dim(block, block.shape[dim] - width, None, axis...  23.7 us
    ppermute x8, starting transfers between devices, padded_2(): lax.ppermute(lax.slice_in_dim(block, block.shape[dim] - width, None, axis...  16.3 us
    another operation x14, local copies, waits for them, and re-layouts, tiled(): return jnp.tile(values, (1, 1, count_rhs))  16.1 us
    dot_general x6, matrix products, block_gram(): return jnp.einsum('psz,ptz->st', left, right, precision=HIGH)  14 us
  transfers between devices with their start and end apart: 18, of which 6 were waited for; matrix products, arithmetic and copies ran while one was open for 5% of the time, Pallas kernels for 0%

commit v1 on v0

--- a/solution.py
+++ b/solution.py
@@ -162,7 +162,7 @@
         precond_set.append(upper_sol)
         image_set.append(image)
         local_proj = jnp.stack([block_gram(member, image, count_rhs) for member in basis_set])
-        stacked = lax.psum(local_proj, ("gx", "gy"))
+        stacked = jnp.sum(lax.all_gather(local_proj, ("gx", "gy")), axis=0)
         projections = [stacked[member] for member in range(len(basis_set))]
         removed = mix_block(basis_set[0], projections[0])
         for member in range(1, len(basis_set)):

time: 617 us -> 754 us (1.22)
  blocking collectives: 373 us -> 495 us
  other arithmetic: 44.9 us -> 53.3 us
    all_gather x0 -> x2, blocking collectives: none -> 265 us  [body(): stacked = jnp.sum(lax.all_gather(local_proj, ('gx', 'gy')), axis=0)]
    psum x2 -> x0, blocking collectives: 146 us -> none  [body(): stacked = lax.psum(local_proj, ('gx', 'gy'))]
  transfers between devices with their start and end apart: 18 -> 18, of which waited for: 6 -> 6; matrix products, arithmetic and copies ran while one was open for 5% -> 4% of each run, Pallas kernels for 0% -> 0%
where the time goes in v1:
time: 754 us; the launch traced here: 746 us
  blocking collectives  495 us (66%)
  local copies, waits for them, and re-layouts  87.1 us (12%)
  starting transfers between devices  54.8 us (7%)
  other arithmetic  53.3 us (7%)
  matrix products  30.4 us (4%)
  waiting for transfers between devices  24.1 us (3%)
    all_gather x2, blocking collectives, body(): stacked = jnp.sum(lax.all_gather(local_proj, ('gx', 'gy')), axis=0)  265 us
    psum x3, blocking collectives, total_gram(): return lax.psum(block_gram(former, latter, count_rhs), ('gx', 'gy'))  229 us
    ppermute x8, starting transfers between devices, padded_2(): lax.ppermute(lax.slice_in_dim(block, 0, width, axis=dim), axis, backward)  33.8 us
    ppermute x8, waiting for transfers between devices, padded_2(): lax.ppermute(lax.slice_in_dim(block, block.shape[dim] - width, None, axis...  24 us
    another operation x14, local copies, waits for them, and re-layouts, tiled(): return jnp.tile(values, (1, 1, count_rhs))  16.9 us
    ppermute x8, starting transfers between devices, padded_2(): lax.ppermute(lax.slice_in_dim(block, block.shape[dim] - width, None, axis...  15.4 us
  transfers between devices with their start and end apart: 18, of which 6 were waited for; matrix products, arithmetic and copies ran while one was open for 4% of the time, Pallas kernels for 0%

profile of v1, /device:TPU:40, one launch (start us, length us, event | category | flops | bytes accessed | tf_op | source)
XLA Modules:
  0.0 745.9 jit_solution(17148361328216369678)
XLA Ops:
  3.4 3.6 collective-permute-start.2
  10.8 3.4 collective-permute-start.1
  32.1 4.6 collective-permute-start.4
  42.0 3.6 collective-permute-done.5
  45.6 3.9 fusion.36
  51.8 3.1 convolution_bitcast_fusion.12
  54.9 2.5 copy.56
  60.1 77.2 %psum.21 = f32[16,16]{0,1:T(8,128)S(1)} all-reduce(f32[16,16]{0,1:T(8,128)S(1)} %convolution_bitcast_fusion.12), channel_id=1, replica_groups=mesh['gx'=16,'gy'=16] {'gx','gy'}, use_global_device_ids=true, to_apply=%region_0.1 | all-reduce | flops 256 | bytes 2048 | tf_op jit(solution)/shard_map/psum | solution.py:136
  154.7 2.8 collective-permute-start.6
  159.4 3.3 collective-permute-done.7
  162.8 4.6 collective-permute-start.8
  169.6 6.2 collective-permute-done.9
  179.6 2.5 copy.58
  184.1 122.7 %all-gather = f32[4096,16]{1,0:T(8,128)} all-gather(f32[16,16]{1,0:T(8,128)S(1)} %convolution_bitcast_fusion.10), channel_id=2, replica_groups=mesh['gx'=16,'gy'=16] {'gx','gy'}, dimensions={0}, use_global_device_ids=true | all-gather | bytes 263168 | tf_op jit(solution)/shard_map/all_gather | solution.py:165
  322.9 3.1 convolution_bitcast_fusion.9
  326.0 76.0 %psum.22 = f32[16,16]{0,1:T(8,128)S(1)} all-reduce(f32[16,16]{0,1:T(8,128)S(1)} %convolution_bitcast_fusion.9), channel_id=1, replica_groups=mesh['gx'=16,'gy'=16] {'gx','gy'}, use_global_device_ids=true, to_apply=%region_4.7 | all-reduce | flops 256 | bytes 2048 | tf_op jit(solution)/shard_map/psum | solution.py:136
  421.8 4.8 collective-permute-start.10
  430.8 2.5 copy.74
  434.8 4.6 collective-permute-start.12
  443.9 2.5 copy.76
  447.8 2.9 fusion.15
  453.1 2.5 copy.66
  459.4 142.5 %all-gather.1 = f32[512,16,16]{2,1,0:T(8,128)} all-gather(f32[2,16,16]{2,1,0:T(8,128)S(1)} %pad_maximum_fusion.39), channel_id=3, replica_groups=mesh['gx'=16,'gy'=16] {'gx','gy'}, dimensions={0}, use_global_device_ids=true | all-gather | bytes 526336 | tf_op jit(solution)/shard_map/all_gather | solution.py:165
  602.0 2.5 reduce_sum.19
  614.0 3.1 convolution_bitcast_fusion.5
  617.1 76.1 %psum.23 = f32[16,16]{0,1:T(8,128)S(1)} all-reduce(f32[16,16]{0,1:T(8,128)S(1)} %convolution_bitcast_fusion.5), channel_id=1, replica_groups=mesh['gx'=16,'gy'=16] {'gx','gy'}, use_global_device_ids=true, to_apply=%region_6.9 | all-reduce | flops 256 | bytes 2048 | tf_op jit(solution)/shard_map/psum | solution.py:136
  697.4 2.9 cholesky.41
  720.4 4.1 collective-permute-start.14
  726.5 3.3 collective-permute-done.15
  729.9 4.6 collective-permute-start.16
  736.7 6.2 collective-permute-done.17
  742.9 2.8 fusion.5
  (227 shorter events, 152.7 us)
Async XLA Ops:
  0.6 18.4 %copy-start.16 = (f32[16,8,64]{2,1,0:T(8,128)S(1)}, f32[16,8,64]{2,1,0:T(8,128)}, u32[]{:S(2)}) copy-start(f32[16,8,64]{2,1,0:T(8,128)} %param.11) | copy-start | bytes 98308
  0.6 18.0 %copy-start.15 = (f32[16,8,64]{2,1,0:T(8,128)S(1)}, f32[16,8,64]{2,1,0:T(8,128)}, u32[]{:S(2)}) copy-start(f32[16,8,64]{2,1,0:T(8,128)} %param.12) | copy-start | bytes 98308
  1.5 29.6 %collective-permute-start.3 = (f32[1,8,1024]{2,1,0:T(8,128)S(1)}, f32[1,8,1024]{2,1,0:T(8,128)S(1)}, u32[]{:S(2)}, u32[]{:S(2)}) collective-permute-start(f32[1,8,1024]{2,1,0:T(8,128)S(1)} %get-tuple-element.31), channel_id=1, source_target_pairs={{0,16},{16,32},{32,48},{48,64},{64,80},{80,96},{96,112},{112,128},... | collective-permute-start | bytes 98312 | tf_op jit(solution)/shard_map/ppermute | solution.py:23
  3.4 27.7 %collective-permute-start.2 = (f32[1,8,1024]{2,1,0:T(8,128)S(1)}, f32[1,8,1024]{2,1,0:T(8,128)S(1)}, u32[]{:S(2)}, u32[]{:S(2)}) collective-permute-start(f32[1,8,1024]{2,1,0:T(8,128)S(1)} %get-tuple-element.30), channel_id=1, source_target_pairs={{16,0},{32,16},{48,32},{64,48},{80,64},{96,80},{112,96},{128,112},... | collective-permute-start | bytes 98312 | tf_op jit(solution)/shard_map/ppermute | solution.py:26
  7.7 19.9 %collective-permute-start = (f32[1,8,64]{2,1,0:T(8,128)S(1)}, f32[1,8,64]{2,1,0:T(8,128)S(1)}, u32[]{:S(2)}, u32[]{:S(2)}) collective-permute-start(f32[1,8,64]{2,1,0:T(8,128)S(1)} %slice.369), channel_id=1, source_target_pairs={{0,16},{16,32},{32,48},{48,64},{64,80},{80,96},{96,112},{112,128},... | collective-permute-start | bytes 6152 | tf_op jit(solution)/shard_map/ppermute | solution.py:15
  10.8 27.8 %collective-permute-start.1 = (f32[16,1,64]{2,1,0:T(1,128)S(1)}, f32[16,1,64]{2,1,0:T(1,128)S(1)}, u32[]{:S(2)}, u32[]{:S(2)}) collective-permute-start(f32[16,1,64]{2,1,0:T(1,128)S(1)} %slice.371), channel_id=1, source_target_pairs={{0,1},{1,2},{2,3},{3,4},{4,5},{5,6},{6,7},{7,8},{8,9},{9,10},{10,1... | collective-permute-start | bytes 12296 | tf_op jit(solution)/shard_map/ppermute | solution.py:15
  16.5 5.1 copy-start.17
  21.7 9.4 %copy-start.7 = (f32[16,8,1024]{2,1,0:T(8,128)S(1)}, f32[16,8,1024]{2,1,0:T(8,128)}, u32[]{:S(2)}) copy-start(f32[16,8,1024]{2,1,0:T(8,128)} %param.10) | copy-start | bytes 1572868
  32.1 9.9 %collective-permute-start.4 = (f32[18,1,1024]{2,1,0:T(1,128)S(1)}, f32[18,1,1024]{2,1,0:T(1,128)S(1)}, u32[]{:S(2)}, u32[]{:S(2)}) collective-permute-start(f32[18,1,1024]{2,1,0:T(1,128)S(1)} %get-tuple-element.14), channel_id=1, source_target_pairs={{1,0},{2,1},{3,2},{4,3},{5,4},{6,5},{7,6},{8,7},{9,8},{10,9},{11,1... | collective-permute-start | bytes 221192 | tf_op jit(solution)/shard_map/ppermute | solution.py:26
  36.6 8.9 %collective-permute-start.5 = (f32[18,1,1024]{2,1,0:T(1,128)S(1)}, f32[18,1,1024]{2,1,0:T(1,128)S(1)}, u32[]{:S(2)}, u32[]{:S(2)}) collective-permute-start(f32[18,1,1024]{2,1,0:T(1,128)S(1)} %get-tuple-element.15), channel_id=1, source_target_pairs={{0,1},{1,2},{2,3},{3,4},{4,5},{5,6},{6,7},{7,8},{8,9},{9,10},{10,1... | collective-permute-start | bytes 221192 | tf_op jit(solution)/shard_map/ppermute | solution.py:23
  143.4 3.8 copy-start.3
  154.1 21.7 %copy-start.10 = (f32[16,8,1024]{2,1,0:T(8,128)S(1)}, f32[16,8,1024]{2,1,0:T(8,128)}, u32[]{:S(2)}) copy-start(f32[16,8,1024]{2,1,0:T(8,128)} %tile.63) | copy-start | bytes 1572868
  154.1 21.7 %copy-start.11 = (f32[16,8,1024]{2,1,0:T(8,128)S(1)}, f32[16,8,1024]{2,1,0:T(8,128)}, u32[]{:S(2)}) copy-start(f32[16,8,1024]{2,1,0:T(8,128)} %tile.67) | copy-start | bytes 1572868
  154.6 21.2 %copy-start = (f32[16,8,1024]{2,1,0:T(8,128)}, f32[16,8,1024]{2,1,0:T(8,128)S(1)}, u32[]{:S(2)}) copy-start(f32[16,8,1024]{2,1,0:T(8,128)S(1)} %multiply_add_fusion.4) | copy-start | bytes 1572868
  154.7 4.8 collective-permute-start.6
  157.5 5.2 collective-permute-start.7
  162.8 6.8 collective-permute-start.8
  167.5 8.4 %collective-permute-start.9 = (f32[18,1,1024]{2,1,0:T(1,128)S(1)}, f32[18,1,1024]{2,1,0:T(1,128)S(1)}, u32[]{:S(2)}, u32[]{:S(2)}) collective-permute-start(f32[18,1,1024]{2,1,0:T(1,128)S(1)} %get-tuple-element.13), channel_id=1, source_target_pairs={{0,1},{1,2},{2,3},{3,4},{4,5},{5,6},{6,7},{7,8},{8,9},{9,10},{10,1... | collective-permute-start | bytes 221192 | tf_op jit(solution)/shard_map/ppermute | solution.py:23
  413.5 2.8 copy-start.6
  421.8 19.5 %copy-start.2 = (f32[16,8,1024]{2,1,0:T(8,128)S(1)}, f32[16,8,1024]{2,1,0:T(8,128)}, u32[]{:S(2)}) copy-start(f32[16,8,1024]{2,1,0:T(8,128)} %copy-done.1) | copy-start | bytes 1572868
  421.8 11.5 %collective-permute-start.10 = (f32[1,8,1024]{2,1,0:T(8,128)S(1)}, f32[1,8,1024]{2,1,0:T(8,128)S(1)}, u32[]{:S(2)}, u32[]{:S(2)}) collective-permute-start(f32[1,8,1024]{2,1,0:T(8,128)S(1)} %get-tuple-element.23), channel_id=1, source_target_pairs={{16,0},{32,16},{48,32},{64,48},{80,64},{96,80},{112,96},{128,112},... | collective-permute-start | bytes 98312 | tf_op jit(solution)/shard_map/ppermute | solution.py:26
  426.6 6.8 collective-permute-start.11
  434.8 11.6 %collective-permute-start.12 = (f32[18,1,1024]{2,1,0:T(1,128)S(1)}, f32[18,1,1024]{2,1,0:T(1,128)S(1)}, u32[]{:S(2)}, u32[]{:S(2)}) collective-permute-start(f32[18,1,1024]{2,1,0:T(1,128)S(1)} %get-tuple-element.10), channel_id=1, source_target_pairs={{1,0},{2,1},{3,2},{4,3},{5,4},{6,5},{7,6},{8,7},{9,8},{10,9},{11,1... | collective-permute-start | bytes 221192 | tf_op jit(solution)/shard_map/ppermute | solution.py:26
  439.4 8.4 %collective-permute-start.13 = (f32[18,1,1024]{2,1,0:T(1,128)S(1)}, f32[18,1,1024]{2,1,0:T(1,128)S(1)}, u32[]{:S(2)}, u32[]{:S(2)}) collective-permute-start(f32[18,1,1024]{2,1,0:T(1,128)S(1)} %get-tuple-element.11), channel_id=1, source_target_pairs={{0,1},{1,2},{2,3},{3,4},{4,5},{5,6},{6,7},{7,8},{8,9},{9,10},{10,1... | collective-permute-start | bytes 221192 | tf_op jit(solution)/shard_map/ppermute | solution.py:23
  450.7 6.9 copy-start.12
  459.4 145.1 %copy-start.4 = (f32[128,16,64]{0,1,2:T(8,128)S(1)}, f32[128,16,64]{0,1,2:T(8,128)}, u32[]{:S(2)}) copy-start(f32[128,16,64]{0,1,2:T(8,128)} %copy-done.3) | copy-start | bytes 1572868
  704.5 14.6 %copy-start.8 = (f32[16,8,1024]{2,1,0:T(8,128)S(1)}, f32[16,8,1024]{2,1,0:T(8,128)}, u32[]{:S(2)}) copy-start(f32[16,8,1024]{2,1,0:T(8,128)} %param.10) | copy-start | bytes 1572868
  720.4 25.3 %copy-start.9 = (f32[16,8,1024]{2,1,0:T(8,128)}, f32[16,8,1024]{2,1,0:T(8,128)S(1)}, u32[]{:S(2)}) copy-start(f32[16,8,1024]{2,1,0:T(8,128)S(1)} %add_add_fusion) | copy-start | bytes 1572868
  720.4 6.1 collective-permute-start.14
  724.5 5.2 collective-permute-start.15
  729.9 6.8 collective-permute-start.16
  734.5 8.4 %collective-permute-start.17 = (f32[18,1,1024]{2,1,0:T(1,128)S(1)}, f32[18,1,1024]{2,1,0:T(1,128)S(1)}, u32[]{:S(2)}, u32[]{:S(2)}) collective-permute-start(f32[18,1,1024]{2,1,0:T(1,128)S(1)} %get-tuple-element.9), channel_id=1, source_target_pairs={{0,1},{1,2},{2,3},{3,4},{4,5},{5,6},{6,7},{7,8},{8,9},{9,10},{10,1... | collective-permute-start | bytes 221192 | tf_op jit(solution)/shard_map/ppermute | solution.py:23
  (4 other events, 4.6 us)
